TPU v7x, 512 devices: a whole 4x4x16 slice. The times are simulated.
512 devices in a mesh: expert: 8 (over y, core), mp: 64 (over x, z).
Axes of the slice: x: 4, y: 4, z: 16, core: 2. Of those that a mesh axis runs over, the one named last changes fastest.
Arguments:
- context: bfloat16 [4096, 2048], P('expert', 'mp'), may hold values from -6 to 6
- out_proj: bfloat16 [2048, 2048], P('mp'), may hold values from -1 to 1, as said below
- routes: int32 [4096, 2], P('expert'), may hold values from 0 to 7, all different within a row; in each aligned block of 512 rows (0 to 511, 512 to 1023, ...) at most 256 rows name the same one
- router_logits: float32 [4096, 2], P('expert'), may hold values from -8 to 8
- w_gate: bfloat16 [45056, 2048], P('mp', 'expert'), may hold values from -0.125 to 0.125
- w_up: bfloat16 [45056, 2048], P('mp', 'expert'), may hold values from -0.125 to 0.125
- w_down: bfloat16 [45056, 2048], P('mp', 'expert'), may hold values from -0.078125 to 0.078125
- norm_gain: float32 [2048], P('mp'), may hold values from 0.25 to 1.75
- request_order: int32 [4096], P('expert'), may hold values from 0 to 4095, each once
Outputs:
- restored: bfloat16 [4096, 2048], P('expert', 'mp')
Inputs may be any that keep to these rules, and one draw needn't show every extreme that they name: `routes`: each row names 2 different experts. Within each aligned block of 512 rows no expert is named by more than 256 rows, and in some blocks one expert is named by exactly 256 rows. `request_order`: A permutation of the 4096 token rows. `out_proj`: entries of the order of one over the square root of 2048.
All inputs are finite; a program needn't handle non-finite values.
Results may differ from a plain program's by a relative error of at most 0.0056.
Values may be sent and summed in bfloat16 or wider, within the bound.
No kernel may reach another device: no remote copies, remote signals or barrier semaphores. Data moves between devices by JAX's collectives and lax.ppermute only.
A program may use at most 64 MiB of HBM per device.

v0:
```python
import jax
import jax.numpy as jnp
from jax import lax
from jax.sharding import PartitionSpec as P

EXPERTS = 8
CAP = 256
epsilon = 1e-06


def slot_targets(routes, capacity, experts):
    flat_routes = routes.reshape(-1)
    onehot = (flat_routes[:, None] == jnp.arange(experts, dtype=jnp.int32)[None, :]).astype(
        jnp.int32
    )
    earlier = jnp.cumsum(onehot, axis=0) - onehot
    slot_index = jnp.sum(earlier * onehot, axis=1)
    return flat_routes * capacity + slot_index


def shards(
    context, out_proj, routes, router_logits, w_gate, w_up, w_down, norm_gain, request_order
):
    tok_rows = context.shape[0]
    feat_local = context.shape[1]
    model_width = out_proj.shape[1]
    mp_count = lax.axis_size("mp")
    copies = mp_count // EXPERTS
    capacity = CAP
    top_k = routes.shape[1]
    attended = jnp.einsum(
        "td,cd->tc",
        lax.all_gather(context, "mp", axis=1, tiled=True),
        out_proj,
        preferred_element_type=jnp.float32,
    ).astype(jnp.bfloat16)
    destination = slot_targets(routes, capacity, EXPERTS)
    source_rows = jnp.repeat(jnp.arange(tok_rows, dtype=jnp.int32), top_k)
    slotted = (
        jnp.zeros((EXPERTS * capacity, feat_local), jnp.bfloat16)
        .at[destination]
        .set(attended[source_rows])
    )
    slotted = jnp.repeat(slotted.reshape(EXPERTS, capacity, feat_local), copies, axis=0)
    outgoing = slotted.transpose(1, 0, 2).reshape(capacity, mp_count * feat_local)
    inbox_rows = lax.all_to_all(outgoing, "mp", split_axis=1, concat_axis=1, tiled=True)
    gate_next = jnp.einsum(
        "rd,hd->rh",
        inbox_rows,
        lax.all_gather(w_gate, "expert", axis=1, tiled=True),
        preferred_element_type=jnp.float32,
    )
    up_next = jnp.einsum(
        "rd,hd->rh",
        inbox_rows,
        lax.all_gather(w_up, "expert", axis=1, tiled=True),
        preferred_element_type=jnp.float32,
    )
    activated = (jax.nn.silu(gate_next) * up_next).astype(jnp.bfloat16)
    partial_value = jnp.dot(
        activated,
        lax.all_gather(w_down, "expert", axis=1, tiled=True),
        preferred_element_type=jnp.float32,
    )
    returned = lax.all_to_all(partial_value, "mp", split_axis=1, concat_axis=0, tiled=True)
    expert_out = jnp.sum(returned.reshape(EXPERTS, copies, capacity, feat_local), axis=1).reshape(
        EXPERTS * capacity, feat_local
    )
    picked = expert_out[destination].reshape(tok_rows, top_k, feat_local)
    weights = 1.0 / (1.0 + jnp.exp(router_logits[:, ::-1] - router_logits))
    branch = jnp.sum(picked * weights[:, :, None], axis=1)
    combined = attended.astype(jnp.float32) + branch
    squares = lax.psum(jnp.sum(combined * combined, axis=1), "mp")
    normed = (
        combined * norm_gain[None, :] * lax.rsqrt(squares / model_width + epsilon)[:, None]
    ).astype(jnp.bfloat16)
    everyone = lax.all_gather(normed, "expert", axis=0, tiled=True)
    return everyone[request_order]


def solution(mesh):
    placed = (
        P("expert", "mp"),
        P("mp", None),
        P("expert", None),
        P("expert", None),
        P("mp", "expert"),
        P("mp", "expert"),
        P("mp", "expert"),
        P("mp"),
        P("expert"),
    )
    return jax.shard_map(
        shards, mesh=mesh, in_specs=placed, out_specs=P("expert", "mp"), check_vma=False
    )
```

profile of v0, /device:TPU:1, one launch (start us, length us, event | category | flops | bytes accessed | tf_op | source)
XLA Modules:
  0.0 565.7 jit_solution(14208333560372502879)
XLA Ops:
  6.5 0.0 copy-start
  6.5 0.0 all-gather.5.cloned.1.call-start
  6.5 0.7 all-gather.5.cloned.1.call-update
  7.3 0.0 all-gather.7.cloned.1.call-start
  7.3 0.7 all-gather.7.cloned.1.call-update
  8.0 0.0 all-gather.11.cloned.1.call-start
  8.1 0.7 all-gather.11.cloned.1.call-update
  8.7 0.0 all-gather.9.cloned.1.call-start
  8.8 0.5 all-gather.9.cloned.1.call-update
  9.3 0.8 copy.42
  10.2 0.2 eq.29
  10.3 0.2 eq.25
  10.5 0.7 broadcast_multiply_fusion
  11.2 2.3 reduce-window.6
  13.5 0.3 slice_reduce_fusion
  13.7 0.2 reduce-window.9
  13.9 0.1 add_bitcast_fusion
  14.0 0.2 copy.41
  14.1 0.2 mul.55
  14.4 0.2 reshape.104
  14.6 133.1 %all-gather.5.cloned.1.call-done = bf16[512,2048]{0,1:T(8,128)(2,1)} async-done(((bf16[512,32]{0,1:T(8,128)(2,1)}), bf16[512,2048]{0,1:T(8,128)(2,1)}) %all-gather.5.cloned.1.call-update) | async-done | bytes 2097168 | tf_op jit(solution)/shard_map/all_gather | solution.py:33
  147.7 0.0 copy-done
  147.7 2.0 convolution_convert_fusion
  149.7 0.1 copy.44
  149.9 6.4 %scatter_custom_fusion = bf16[2048,32]{1,0:T(8,128)(2,1)S(1)} fusion(s32[1024]{0:T(1024)S(1)} %bitcast.48, bf16[512,32]{1,0:T(8,128)(2,1)S(1)} %copy.44, s32[1024]{0:T(1024)S(1)} %broadcast_clamp_fusion.1, bf16[]{:T(256)} %constant.10.clone.1), kind=kCustom, calls=%fused_computation.16 | custom fusion | bytes 131074 | tf_op jit(solution)/shard_map/scatter | solution.py:42
  156.3 0.2 copy.46
  156.5 1.2 broadcast_in_dim.10
  157.7 8.8 %all-to-all-start = ((bf16[256,64,32]{0,2,1:T(8,128)(2,1)}), bf16[256,64,32]{0,2,1:T(8,128)(2,1)S(1)}, u32[]{:S(2)}, u32[]{:S(2)}) async-start(bf16[256,64,32]{0,2,1:T(8,128)(2,1)} %bitcast.6), calls=%async_computation | async-start | bytes 2097152 | tf_op jit(solution)/shard_map/all_to_all | solution.py:46
  166.5 26.9 %all-gather.7.cloned.1.call-done = bf16[704,2048]{1,0:T(8,128)(2,1)} async-done(((bf16[704,256]{1,0:T(8,128)(2,1)}), bf16[704,2048]{1,0:T(8,128)(2,1)}) %all-gather.7.cloned.1.call-update) | async-done | bytes 2883600 | tf_op jit(solution)/shard_map/all_gather | solution.py:50
  193.4 12.3 %all-to-all-done = bf16[256,64,32]{0,2,1:T(8,128)(2,1)S(1)} async-done(((bf16[256,64,32]{0,2,1:T(8,128)(2,1)}), bf16[256,64,32]{0,2,1:T(8,128)(2,1)S(1)}, u32[]{:S(2)}, u32[]{:S(2)}) %all-to-all-start) | async-done | bytes 1048608 | tf_op jit(solution)/shard_map/all_to_all | solution.py:46
  205.6 2.7 fusion.16
  208.4 26.4 %all-gather.11.cloned.1.call-done = bf16[704,2048]{1,0:T(8,128)(2,1)} async-done(((bf16[704,256]{1,0:T(8,128)(2,1)}), bf16[704,2048]{1,0:T(8,128)(2,1)}) %all-gather.11.cloned.1.call-update) | async-done | bytes 2883600 | tf_op jit(solution)/shard_map/all_gather | solution.py:62
  234.8 41.3 %all-gather.9.cloned.1.call-done = bf16[704,2048]{1,0:T(8,128)(2,1)} async-done(((bf16[704,256]{1,0:T(8,128)(2,1)}), bf16[704,2048]{1,0:T(8,128)(2,1)}) %all-gather.9.cloned.1.call-update) | async-done | bytes 2883600 | tf_op jit(solution)/shard_map/all_gather | solution.py:56
  276.1 7.2 %fusion.1 = f32[256,2048]{0,1:T(8,128)} fusion(bf16[704,2048]{1,0:T(8,128)(2,1)} %all-gather.11.cloned.1.call-done, bf16[704,2048]{1,0:T(8,128)(2,1)} %all-gather.9.cloned.1.call-done, bf16[256,2048]{0,1:T(8,128)(2,1)S(1)} %bitcast.46, f32[256,704]{0,1:T(8,128)S(1)} %fusion.16), kind=kOutput, calls=%fused_computation.8 | convolution fusion | flops 1477476352 | bytes 9633792 | tf_op jit(solution)/shard_map/dot_general | solution.py:60
  283.4 0.0 copy-start.1
  283.4 0.0 copy-start.2
  283.4 15.6 %all-to-all-start.1 = ((f32[256,64,32]{0,2,1:T(8,128)}), f32[256,64,32]{0,2,1:T(8,128)S(1)}, u32[]{:S(2)}, u32[]{:S(2)}) async-start(f32[256,64,32]{0,2,1:T(8,128)} %bitcast.43), calls=%async_computation.1 | async-start | bytes 4194304 | tf_op jit(solution)/shard_map/all_to_all | solution.py:65
  299.0 0.0 copy-done.1
  299.0 0.1 rev.3
  299.2 0.1 copy.49
  299.3 0.0 copy-done.2
  299.4 91.4 %all-to-all-done.1 = f32[256,64,32]{0,2,1:T(8,128)S(1)} async-done(((f32[256,64,32]{0,2,1:T(8,128)}), f32[256,64,32]{0,2,1:T(8,128)S(1)}, u32[]{:S(2)}, u32[]{:S(2)}) %all-to-all-start.1) | async-done | bytes 2097184 | tf_op jit(solution)/shard_map/all_to_all | solution.py:65
  390.8 0.2 bitcast_reduce_fusion
  390.9 0.3 copy.48
  391.3 0.0 copy-start.3
  391.3 2.8 gather_fusion
  394.1 2.8 multiply_reduce_fusion
  396.9 0.1 copy.50
  397.1 118.5 %psum.7 = f32[512]{0:T(512)S(1)} all-reduce(f32[512]{0:T(512)S(1)} %multiply_reduce_fusion.1), channel_id=1, replica_groups=mesh['expert'=8,'mp'=64] {'mp'}, use_global_device_ids=true, to_apply=%region_7.8 | all-reduce | flops 512 | bytes 4096 | tf_op jit(solution)/shard_map/psum | solution.py:73
  515.5 0.0 copy-done.3
  515.6 0.1 multiply_convert_fusion
  515.6 41.0 %all_gather.19 = bf16[4096,32]{0,1:T(8,128)(2,1)S(1)} all-gather(bf16[512,32]{0,1:T(8,128)(2,1)S(1)} %multiply_convert_fusion), channel_id=1, replica_groups=mesh['expert'=8,'mp'=64] {'expert'}, dimensions={0}, use_global_device_ids=true | all-gather | bytes 294912 | tf_op jit(solution)/shard_map/all_gather | solution.py:77
  556.6 0.5 copy.51
  557.1 1.3 gather_fusion.1
  558.4 0.7 copy.52
  (12 shorter events, 0.1 us)
Async XLA Ops:
  6.5 141.2 %copy-start = (bf16[32,2048]{1,0:T(8,128)(2,1)S(1)}, bf16[32,2048]{1,0:T(8,128)(2,1)}, u32[]{:S(2)}) copy-start(bf16[32,2048]{1,0:T(8,128)(2,1)} %param.10) | copy-start | bytes 393220
  6.5 141.2 %all-gather.5.cloned.1.call-start = ((), (), s32[]{:S(2)}) async-start(), calls=%async_computation.2 | async-start | bytes 2129920 | tf_op jit(solution)/shard_map/all_gather | solution.py:33
  7.3 186.1 %all-gather.7.cloned.1.call-start = ((), (), s32[]{:S(2)}) async-start(), calls=%async_computation.3 | async-start | bytes 3244032 | tf_op jit(solution)/shard_map/all_gather | solution.py:50
  8.0 226.8 %all-gather.11.cloned.1.call-start = ((), (), s32[]{:S(2)}) async-start(), calls=%async_computation.5 | async-start | bytes 3244032 | tf_op jit(solution)/shard_map/all_gather | solution.py:62
  8.7 267.4 %all-gather.9.cloned.1.call-start = ((), (), s32[]{:S(2)}) async-start(), calls=%async_computation.4 | async-start | bytes 3244032 | tf_op jit(solution)/shard_map/all_gather | solution.py:56
  157.7 48.0 %all-to-all-start = ((bf16[256,64,32]{0,2,1:T(8,128)(2,1)}), bf16[256,64,32]{0,2,1:T(8,128)(2,1)S(1)}, u32[]{:S(2)}, u32[]{:S(2)}) async-start(bf16[256,64,32]{0,2,1:T(8,128)(2,1)} %bitcast.6), calls=%async_computation | async-start | bytes 2097152 | tf_op jit(solution)/shard_map/all_to_all | solution.py:46
  283.4 15.7 %copy-start.1 = (f32[512,2]{0,1:T(2,128)S(1)}, f32[512,2]{0,1:T(2,128)}, u32[]{:S(2)}) copy-start(f32[512,2]{0,1:T(2,128)} %param.12) | copy-start | bytes 12292
  283.4 16.0 %copy-start.2 = (s32[512]{0:T(512)S(1)}, s32[512]{0:T(512)}, u32[]{:S(2)}) copy-start(s32[512]{0:T(512)} %param.17) | copy-start | bytes 6148
  283.4 107.4 %all-to-all-start.1 = ((f32[256,64,32]{0,2,1:T(8,128)}), f32[256,64,32]{0,2,1:T(8,128)S(1)}, u32[]{:S(2)}, u32[]{:S(2)}) async-start(f32[256,64,32]{0,2,1:T(8,128)} %bitcast.43), calls=%async_computation.1 | async-start | bytes 4194304 | tf_op jit(solution)/shard_map/all_to_all | solution.py:65
  391.3 124.3 %copy-start.3 = (f32[32]{0:T(128)S(1)}, f32[32]{0:T(128)}, u32[]{:S(2)}) copy-start(f32[32]{0:T(128)} %param.16) | copy-start | bytes 388
Sparse Core Ops, SparseCore 0:
  10.3 137.3 all-gather.4
  149.8 43.5 all-gather.6
  195.5 39.2 all-gather.10
  236.8 39.2 all-gather.8
where the time goes:
time: 566 us
  waiting for transfers between devices  334 us (59%)
  blocking collectives  159 us (28%)
  starting transfers between devices  24.5 us (4%)
  local copies, waits for them, and re-layouts  16 us (3%)
  between operations  13.4 us (2%)
  matrix products  12 us (2%)
  other arithmetic  6.35 us (1%)
    all_gather x1, waiting for transfers between devices, shards(): lax.all_gather(context, 'mp', axis=1, tiled=True)  133 us
    psum x1, blocking collectives, shards(): squares = lax.psum(jnp.sum(combined * combined, axis=1), 'mp')  118 us
    all_to_all x1, waiting for transfers between devices, shards(): lax.all_to_all(partial_value, 'mp', split_axis=1, concat_axis=0, tiled=True)  91.4 us
    all_gather x1, waiting for transfers between devices, shards(): lax.all_gather(w_up, 'expert', axis=1, tiled=True)  41.3 us
    all_gather x1, blocking collectives, shards(): everyone = lax.all_gather(normed, 'expert', axis=0, tiled=True)  41 us
    all_gather x1, waiting for transfers between devices, shards(): lax.all_gather(w_gate, 'expert', axis=1, tiled=True)  26.9 us
    all_gather x1, waiting for transfers between devices, shards(): lax.all_gather(w_down, 'expert', axis=1, tiled=True)  26.4 us
    all_to_all x1, starting transfers between devices, shards(): lax.all_to_all(partial_value, 'mp', split_axis=1, concat_axis=0, tiled=True)  15.6 us
  transfers between devices with their start and end apart: 6, of which 6 were waited for; matrix products, arithmetic and copies ran while one was open for 3% of the time, Pallas kernels for 0%

commit v1 on v0

--- a/solution.py
+++ b/solution.py
@@ -44,12 +44,27 @@
     slotted = jnp.repeat(slotted.reshape(EXPERTS, capacity, feat_local), copies, axis=0)
     outgoing = slotted.transpose(1, 0, 2).reshape(capacity, mp_count * feat_local)
     inbox_rows = lax.all_to_all(outgoing, "mp", split_axis=1, concat_axis=1, tiled=True)
-    gate_next = jnp.einsum(
+    devices, index = (lax.axis_size("expert"), lax.axis_index("expert"))
+    behind = [(i, (i - 1) % devices) for i in range(devices)]
+    rows = w_gate.shape[1]
+    block = w_gate
+    total = jnp.einsum(
         "rd,hd->rh",
-        inbox_rows,
-        lax.all_gather(w_gate, "expert", axis=1, tiled=True),
+        lax.dynamic_slice_in_dim(inbox_rows, index * rows, block.shape[1], axis=1),
+        block,
         preferred_element_type=jnp.float32,
     )
+    for turn in range(1, devices):
+        block = lax.ppermute(block, "expert", behind)
+        total = total + jnp.einsum(
+            "rd,hd->rh",
+            lax.dynamic_slice_in_dim(
+                inbox_rows, (index + turn) % devices * rows, block.shape[1], axis=1
+            ),
+            block,
+            preferred_element_type=jnp.float32,
+        )
+    gate_next = total
     up_next = jnp.einsum(
         "rd,hd->rh",
         inbox_rows,

time: 566 us -> 530 us (0.936)
  waiting for transfers between devices: 334 us -> 270 us
  starting transfers between devices: 24.5 us -> 50.3 us
    ppermute x0 -> x7, waiting for transfers between devices: none -> 42.8 us  [shards(): block = lax.ppermute(block, 'expert', behind)]
    all_gather x1, waiting for transfers between devices: 41.3 us -> 0.02 us  [shards(): lax.all_gather(w_up, 'expert', axis=1, tiled=True)]
    all_gather x1 -> x0, waiting for transfers between devices: 26.9 us -> none  [shards(): lax.all_gather(w_gate, 'expert', axis=1, tiled=True)]
    all_gather x1, waiting for transfers between devices: 26.4 us -> 0.02 us  [shards(): lax.all_gather(w_down, 'expert', axis=1, tiled=True)]
    ppermute x0 -> x7, starting transfers between devices: none -> 25.9 us  [shards(): block = lax.ppermute(block, 'expert', behind)]
    all_to_all x1, waiting for transfers between devices: 12.3 us -> 0.01 us  [shards(): lax.all_to_all(outgoing, 'mp', split_axis=1, concat_axis=1, tiled=True)]
  transfers between devices with their start and end apart: 6 -> 12, of which waited for: 6 -> 8; matrix products, arithmetic and copies ran while one was open for 3% -> 4% of each run, Pallas kernels for 0% -> 0%
where the time goes in v1:
time: 530 us; the launch traced here: 529 us
  waiting for transfers between devices  270 us (51%)
  blocking collectives  160 us (30%)
  starting transfers between devices  50.3 us (9%)
  local copies, waits for them, and re-layouts  17.2 us (3%)
  between operations  13.4 us (3%)
  matrix products  12.4 us (2%)
  other arithmetic  6.36 us (1%)
    all_gather x1, waiting for transfers between devices, shards(): lax.all_gather(context, 'mp', axis=1, tiled=True)  134 us
    psum x1, blocking collectives, shards(): squares = lax.psum(jnp.sum(combined * combined, axis=1), 'mp')  116 us
    all_to_all x1, waiting for transfers between devices, shards(): lax.all_to_all(partial_value, 'mp', split_axis=1, concat_axis=0, tiled=True)  90.4 us
    all_gather x1, blocking collectives, shards(): everyone = lax.all_gather(normed, 'expert', axis=0, tiled=True)  44.4 us
    ppermute x7, waiting for transfers between devices, shards(): block = lax.ppermute(block, 'expert', behind)  42.8 us
    ppermute x7, starting transfers between devices, shards(): block = lax.ppermute(block, 'expert', behind)  25.9 us
    all_to_all x1, starting transfers between devices, shards(): lax.all_to_all(partial_value, 'mp', split_axis=1, concat_axis=0, tiled=True)  15.6 us
  transfers between devices with their start and end apart: 12, of which 8 were waited for; matrix products, arithmetic and copies ran while one was open for 4% of the time, Pallas kernels for 0%

profile of v1, /device:TPU:1, one launch (start us, length us, event | category | flops | bytes accessed | tf_op | source)
XLA Modules:
  0.0 529.4 jit_solution(10407133553343952499)
XLA Ops:
  6.5 0.7 all-gather.4.cloned.1.call-update
  7.3 0.0 all-gather.6.cloned.1.call-start
  7.3 0.7 all-gather.6.cloned.1.call-update
  8.0 0.8 copy.42
  8.8 0.2 eq.37
  9.0 0.2 eq.33
  9.2 2.3 reduce-window.6
  11.5 0.3 slice_reduce_fusion
  11.8 0.2 reduce-window.9
  11.9 0.7 broadcast_multiply_fusion
  12.6 0.1 copy.41
  12.8 0.2 mul.79
  13.0 0.2 reshape.104
  13.2 0.1 add_bitcast_fusion
  13.3 134.4 %all-gather.4.cloned.1.call-done = bf16[512,2048]{0,1:T(8,128)(2,1)} async-done(((bf16[512,32]{0,1:T(8,128)(2,1)}), bf16[512,2048]{0,1:T(8,128)(2,1)}) %all-gather.4.cloned.1.call-update) | async-done | bytes 2097168 | tf_op jit(solution)/shard_map/all_gather | solution.py:33
  147.7 2.0 convolution_convert_fusion
  149.8 0.0 copy-start.4
  149.8 0.1 copy.44
  149.9 0.5 copy-done.2
  150.4 6.4 %scatter_custom_fusion = bf16[2048,32]{1,0:T(8,128)(2,1)S(1)} fusion(s32[1024]{0:T(1024)S(1)} %bitcast.61, bf16[512,32]{1,0:T(8,128)(2,1)S(1)} %copy.44, s32[1024]{0:T(1024)S(1)} %broadcast_clamp_fusion.1, bf16[]{:T(256)} %constant.66.clone.1), kind=kCustom, calls=%fused_computation.17 | custom fusion | bytes 131074 | tf_op jit(solution)/shard_map/scatter | solution.py:42
  156.8 0.2 copy.46
  157.0 1.1 broadcast_in_dim.10
  158.1 8.8 %all-to-all-start = ((bf16[256,64,32]{0,2,1:T(8,128)(2,1)}), bf16[256,64,32]{0,2,1:T(8,128)(2,1)S(1)}, u32[]{:S(2)}, u32[]{:S(2)}) async-start(bf16[256,64,32]{0,2,1:T(8,128)(2,1)} %bitcast.6), calls=%async_computation | async-start | bytes 2097152 | tf_op jit(solution)/shard_map/all_to_all | solution.py:46
  166.9 0.0 all-gather.8.cloned.1.call-start
  167.0 0.7 all-gather.8.cloned.1.call-update
  167.7 11.0 %collective-permute-start = (bf16[704,256]{1,0:T(8,128)(2,1)S(1)}, bf16[704,256]{1,0:T(8,128)(2,1)S(1)}, u32[]{:S(2)}, u32[]{:S(2)}) collective-permute-start(bf16[704,256]{1,0:T(8,128)(2,1)S(1)} %copy-done.4), channel_id=1, source_target_pairs={{0,448},{64,0},{128,64},{192,128},{256,192},{320,256},{384,320},{4... | collective-permute-start | bytes 1081352 | tf_op jit(solution)/shard_map/ppermute | solution.py:58
  178.7 10.5 %collective-permute-done = bf16[704,256]{1,0:T(8,128)(2,1)S(1)} collective-permute-done((bf16[704,256]{1,0:T(8,128)(2,1)S(1)}, bf16[704,256]{1,0:T(8,128)(2,1)S(1)}, u32[]{:S(2)}, u32[]{:S(2)}) %collective-permute-start) | collective-permute-done | bytes 360480 | tf_op jit(solution)/shard_map/ppermute | solution.py:58
  189.2 8.2 %collective-permute-done.1 = bf16[704,256]{1,0:T(8,128)(2,1)S(1)} collective-permute-done((bf16[704,256]{1,0:T(8,128)(2,1)S(1)}, bf16[704,256]{1,0:T(8,128)(2,1)S(1)}, u32[]{:S(2)}, u32[]{:S(2)}) %collective-permute-start.1) | collective-permute-done | bytes 360480 | tf_op jit(solution)/shard_map/ppermute | solution.py:58
  197.3 0.0 collective-permute-start.2
  197.3 7.1 %collective-permute-done.2 = bf16[704,256]{1,0:T(8,128)(2,1)S(1)} collective-permute-done((bf16[704,256]{1,0:T(8,128)(2,1)S(1)}, bf16[704,256]{1,0:T(8,128)(2,1)S(1)}, u32[]{:S(2)}, u32[]{:S(2)}) %collective-permute-start.2) | collective-permute-done | bytes 360480 | tf_op jit(solution)/shard_map/ppermute | solution.py:58
  204.5 7.1 %collective-permute-done.3 = bf16[704,256]{1,0:T(8,128)(2,1)S(1)} collective-permute-done((bf16[704,256]{1,0:T(8,128)(2,1)S(1)}, bf16[704,256]{1,0:T(8,128)(2,1)S(1)}, u32[]{:S(2)}, u32[]{:S(2)}) %collective-permute-start.3) | collective-permute-done | bytes 360480 | tf_op jit(solution)/shard_map/ppermute | solution.py:58
  211.6 1.1 collective-permute-start.4
  212.8 6.0 %collective-permute-done.4 = bf16[704,256]{1,0:T(8,128)(2,1)} collective-permute-done((bf16[704,256]{1,0:T(8,128)(2,1)S(1)}, bf16[704,256]{1,0:T(8,128)(2,1)}, u32[]{:S(2)}, u32[]{:S(2)}) %collective-permute-start.4) | collective-permute-done | bytes 360480 | tf_op jit(solution)/shard_map/ppermute | solution.py:58
  218.8 5.9 %collective-permute-start.5 = (bf16[704,256]{1,0:T(8,128)(2,1)}, bf16[704,256]{1,0:T(8,128)(2,1)S(1)}, u32[]{:S(2)}, u32[]{:S(2)}) collective-permute-start(bf16[704,256]{1,0:T(8,128)(2,1)} %collective-permute-done.4), channel_id=1, source_target_pairs={{0,448},{64,0},{128,64},{192,128},{256,192},{320,256},{384,320},{4... | collective-permute-start | bytes 1081352 | tf_op jit(solution)/shard_map/ppermute | solution.py:58
  224.7 3.9 collective-permute-done.5
  228.5 7.8 %collective-permute-start.6 = (bf16[704,256]{1,0:T(8,128)(2,1)S(1)}, bf16[704,256]{1,0:T(8,128)(2,1)}, u32[]{:S(2)}, u32[]{:S(2)}) collective-permute-start(bf16[704,256]{1,0:T(8,128)(2,1)S(1)} %collective-permute-done.5), channel_id=1, source_target_pairs={{0,448},{64,0},{128,64},{192,128},{256,192},{320,256},{384,320},{4... | collective-permute-start | bytes 1081352 | tf_op jit(solution)/shard_map/ppermute | solution.py:58
  236.4 0.2 fusion.13
  236.6 0.3 convolution_add_fusion.6
  236.9 0.3 convolution_add_fusion.5
  237.2 0.3 convolution_add_fusion.4
  237.4 0.3 convolution_add_fusion.3
  237.7 1.2 convolution_add_fusion.2
  239.0 0.3 convolution_add_fusion.1
  239.2 0.0 all-gather.6.cloned.1.call-done
  239.3 2.8 fusion.29
  242.1 0.0 all-gather.8.cloned.1.call-done
  242.1 4.7 fusion
  246.9 15.6 %all-to-all-start.1 = ((f32[256,64,32]{0,2,1:T(8,128)}), f32[256,64,32]{0,2,1:T(8,128)S(1)}, u32[]{:S(2)}, u32[]{:S(2)}) async-start(f32[256,64,32]{0,2,1:T(8,128)} %bitcast.58), calls=%async_computation.1 | async-start | bytes 4194304 | tf_op jit(solution)/shard_map/all_to_all | solution.py:80
  262.4 0.1 rev.3
  262.6 0.9 copy.49
  263.5 90.4 %all-to-all-done.1 = f32[256,64,32]{0,2,1:T(8,128)S(1)} async-done(((f32[256,64,32]{0,2,1:T(8,128)}), f32[256,64,32]{0,2,1:T(8,128)S(1)}, u32[]{:S(2)}, u32[]{:S(2)}) %all-to-all-start.1) | async-done | bytes 2097184 | tf_op jit(solution)/shard_map/all_to_all | solution.py:80
  353.9 0.2 bitcast_reduce_fusion
  354.0 0.3 copy.48
  354.4 0.0 copy-start.3
  354.4 0.0 copy-start.7
  354.4 2.8 gather_fusion
  357.2 2.8 multiply_reduce_fusion
  360.0 0.1 copy.50
  360.2 115.5 %psum.7 = f32[512]{0:T(512)S(1)} all-reduce(f32[512]{0:T(512)S(1)} %multiply_reduce_fusion.1), channel_id=1, replica_groups=mesh['expert'=8,'mp'=64] {'mp'}, use_global_device_ids=true, to_apply=%region_7.8 | all-reduce | flops 512 | bytes 4096 | tf_op jit(solution)/shard_map/psum | solution.py:88
  475.7 0.1 multiply_convert_fusion.1
  475.8 44.4 %all_gather.15 = bf16[4096,32]{0,1:T(8,128)(2,1)S(1)} all-gather(bf16[512,32]{0,1:T(8,128)(2,1)S(1)} %multiply_convert_fusion.1), channel_id=1, replica_groups=mesh['expert'=8,'mp'=64] {'expert'}, dimensions={0}, use_global_device_ids=true | all-gather | bytes 294912 | tf_op jit(solution)/shard_map/all_gather | solution.py:92
  520.3 0.6 copy.51
  520.8 1.3 gather_fusion.1
  522.2 0.7 copy.52
  (29 shorter events, 0.2 us)
Async XLA Ops:
  6.5 141.2 %copy-start = (bf16[32,2048]{1,0:T(8,128)(2,1)S(1)}, bf16[32,2048]{1,0:T(8,128)(2,1)}, u32[]{:S(2)}) copy-start(bf16[32,2048]{1,0:T(8,128)(2,1)} %param.10) | copy-start | bytes 393220
  6.5 141.2 %all-gather.4.cloned.1.call-start = ((), (), s32[]{:S(2)}) async-start(), calls=%async_computation.2 | async-start | bytes 2129920 | tf_op jit(solution)/shard_map/all_gather | solution.py:33
  7.3 232.0 %all-gather.6.cloned.1.call-start = ((), (), s32[]{:S(2)}) async-start(), calls=%async_computation.3 | async-start | bytes 3244032 | tf_op jit(solution)/shard_map/all_gather | solution.py:71
  149.8 0.6 copy-start.2
  149.8 17.9 %copy-start.4 = (bf16[704,256]{1,0:T(8,128)(2,1)S(1)}, bf16[704,256]{1,0:T(8,128)(2,1)}, u32[]{:S(2)}) copy-start(bf16[704,256]{1,0:T(8,128)(2,1)} %param.13) | copy-start | bytes 1081348
  158.1 78.3 %all-to-all-start = ((bf16[256,64,32]{0,2,1:T(8,128)(2,1)}), bf16[256,64,32]{0,2,1:T(8,128)(2,1)S(1)}, u32[]{:S(2)}, u32[]{:S(2)}) async-start(bf16[256,64,32]{0,2,1:T(8,128)(2,1)} %bitcast.6), calls=%async_computation | async-start | bytes 2097152 | tf_op jit(solution)/shard_map/all_to_all | solution.py:46
  166.9 75.2 %all-gather.8.cloned.1.call-start = ((), (), s32[]{:S(2)}) async-start(), calls=%async_computation.4 | async-start | bytes 3244032 | tf_op jit(solution)/shard_map/all_gather | solution.py:77
  167.7 21.5 %collective-permute-start = (bf16[704,256]{1,0:T(8,128)(2,1)S(1)}, bf16[704,256]{1,0:T(8,128)(2,1)S(1)}, u32[]{:S(2)}, u32[]{:S(2)}) collective-permute-start(bf16[704,256]{1,0:T(8,128)(2,1)S(1)} %copy-done.4), channel_id=1, source_target_pairs={{0,448},{64,0},{128,64},{192,128},{256,192},{320,256},{384,320},{4... | collective-permute-start | bytes 1081352 | tf_op jit(solution)/shard_map/ppermute | solution.py:58
  189.2 8.2 %collective-permute-start.1 = (bf16[704,256]{1,0:T(8,128)(2,1)S(1)}, bf16[704,256]{1,0:T(8,128)(2,1)S(1)}, u32[]{:S(2)}, u32[]{:S(2)}) collective-permute-start(bf16[704,256]{1,0:T(8,128)(2,1)S(1)} %collective-permute-done), channel_id=1, source_target_pairs={{0,448},{64,0},{128,64},{192,128},{256,192},{320,256},{384,320},{4... | collective-permute-start | bytes 1081352 | tf_op jit(solution)/shard_map/ppermute | solution.py:58
  197.3 7.1 %collective-permute-start.2 = (bf16[704,256]{1,0:T(8,128)(2,1)S(1)}, bf16[704,256]{1,0:T(8,128)(2,1)S(1)}, u32[]{:S(2)}, u32[]{:S(2)}) collective-permute-start(bf16[704,256]{1,0:T(8,128)(2,1)S(1)} %collective-permute-done.1), channel_id=1, source_target_pairs={{0,448},{64,0},{128,64},{192,128},{256,192},{320,256},{384,320},{4... | collective-permute-start | bytes 1081352 | tf_op jit(solution)/shard_map/ppermute | solution.py:58
  204.5 7.1 %collective-permute-start.3 = (bf16[704,256]{1,0:T(8,128)(2,1)S(1)}, bf16[704,256]{1,0:T(8,128)(2,1)S(1)}, u32[]{:S(2)}, u32[]{:S(2)}) collective-permute-start(bf16[704,256]{1,0:T(8,128)(2,1)S(1)} %collective-permute-done.2), channel_id=1, source_target_pairs={{0,448},{64,0},{128,64},{192,128},{256,192},{320,256},{384,320},{4... | collective-permute-start | bytes 1081352 | tf_op jit(solution)/shard_map/ppermute | solution.py:58
  211.6 7.1 %collective-permute-start.4 = (bf16[704,256]{1,0:T(8,128)(2,1)S(1)}, bf16[704,256]{1,0:T(8,128)(2,1)}, u32[]{:S(2)}, u32[]{:S(2)}) collective-permute-start(bf16[704,256]{1,0:T(8,128)(2,1)S(1)} %collective-permute-done.3), channel_id=1, source_target_pairs={{0,448},{64,0},{128,64},{192,128},{256,192},{320,256},{384,320},{4... | collective-permute-start | bytes 1081352 | tf_op jit(solution)/shard_map/ppermute | solution.py:58
  218.8 9.8 %collective-permute-start.5 = (bf16[704,256]{1,0:T(8,128)(2,1)}, bf16[704,256]{1,0:T(8,128)(2,1)S(1)}, u32[]{:S(2)}, u32[]{:S(2)}) collective-permute-start(bf16[704,256]{1,0:T(8,128)(2,1)} %collective-permute-done.4), channel_id=1, source_target_pairs={{0,448},{64,0},{128,64},{192,128},{256,192},{320,256},{384,320},{4... | collective-permute-start | bytes 1081352 | tf_op jit(solution)/shard_map/ppermute | solution.py:58
  228.5 13.5 %collective-permute-start.6 = (bf16[704,256]{1,0:T(8,128)(2,1)S(1)}, bf16[704,256]{1,0:T(8,128)(2,1)}, u32[]{:S(2)}, u32[]{:S(2)}) collective-permute-start(bf16[704,256]{1,0:T(8,128)(2,1)S(1)} %collective-permute-done.5), channel_id=1, source_target_pairs={{0,448},{64,0},{128,64},{192,128},{256,192},{320,256},{384,320},{4... | collective-permute-start | bytes 1081352 | tf_op jit(solution)/shard_map/ppermute | solution.py:58
  246.8 15.6 %copy-start.5 = (f32[512,2]{0,1:T(2,128)S(1)}, f32[512,2]{0,1:T(2,128)}, u32[]{:S(2)}) copy-start(f32[512,2]{0,1:T(2,128)} %param.12) | copy-start | bytes 12292
  246.9 16.6 %copy-start.6 = (s32[512]{0:T(512)S(1)}, s32[512]{0:T(512)}, u32[]{:S(2)}) copy-start(s32[512]{0:T(512)} %param.17) | copy-start | bytes 6148
  246.9 107.0 %all-to-all-start.1 = ((f32[256,64,32]{0,2,1:T(8,128)}), f32[256,64,32]{0,2,1:T(8,128)S(1)}, u32[]{:S(2)}, u32[]{:S(2)}) async-start(f32[256,64,32]{0,2,1:T(8,128)} %bitcast.58), calls=%async_computation.1 | async-start | bytes 4194304 | tf_op jit(solution)/shard_map/all_to_all | solution.py:80
  354.0 3.2 copy-start.1
  354.4 5.8 %copy-start.3 = (bf16[512,32]{0,1:T(8,128)(2,1)S(1)}, bf16[512,32]{0,1:T(8,128)(2,1)}, u32[]{:S(2)}) copy-start(bf16[512,32]{0,1:T(8,128)(2,1)} %copy-done.2) | copy-start | bytes 98308
  354.4 121.4 %copy-start.7 = (f32[32]{0:T(128)S(1)}, f32[32]{0:T(128)}, u32[]{:S(2)}) copy-start(f32[32]{0:T(128)} %param.16) | copy-start | bytes 388
Sparse Core Ops, SparseCore 0:
  10.3 137.3 all-gather.3
  149.8 46.4 all-gather.5
  198.5 43.1 all-gather.7
